TPU v7x, 32 devices: a whole 2x2x4 slice. The times are simulated.
32 devices in a mesh: slab: 4 (over x, core), chan: 2 (over y), filt: 4 (over z).
Axes of the slice: x: 2, y: 2, z: 4, core: 2. Of those that a mesh axis runs over, the one named last changes fastest.
Arguments:
- volume: bfloat16 [256, 8, 32, 128], P('chan', 'slab'), may hold values from -6 to 6
- plane_weight: bfloat16 [3, 3, 256, 256], P(None, None, 'chan', 'filt'), may hold values from -0.125 to 0.125
- depth_weight: bfloat16 [3, 256, 256], replicated, may hold values from -0.21875 to 0.21875
- grad_out: bfloat16 [256, 8, 32, 128], P('filt', 'slab', 'chan'), may hold values from -6 to 6
Outputs:
- output: bfloat16 [256, 8, 32, 128], P('filt', 'slab', 'chan')
- grad_in: bfloat16 [256, 8, 32, 128], P('chan', 'slab', 'filt')
All inputs are finite; a program needn't handle non-finite values.
Results may differ from a plain program's by a relative error of at most 0.0049.
Values may be sent and summed in bfloat16 or wider, within the bound.
No kernel may reach another device: no remote copies, remote signals or barrier semaphores. Data moves between devices by JAX's collectives and lax.ppermute only.
A program may use at most 64 MiB of HBM per device.

v0:
```python
import jax
import jax.numpy as jnp
from jax import lax
from jax.sharding import PartitionSpec as P


def with_halo(value, sides, width):
    for axis, dim in sides:
        size, length = (lax.axis_size(axis), value.shape[dim])
        up = [(i, (i + 1) % size) for i in range(size - 1)]
        down = [(j, i) for i, j in up]
        last = lax.slice_in_dim(value, length - width, length, axis=dim)
        leading = lax.slice_in_dim(value, 0, width, axis=dim)
        before = lax.ppermute(last, axis, up)
        after = lax.ppermute(leading, axis, down)
        value = jnp.concatenate([before, value, after], axis=dim)
    return value


def plane_conv(padded, weight):
    rows = padded.shape[2] - 2
    cols = padded.shape[3] - 2
    inputs = weight.shape[2]
    outputs = weight.shape[3]
    total = None
    for row_tap in range(3):
        stacked = jnp.concatenate(
            [
                padded[:, :, row_tap : row_tap + rows, col_tap : col_tap + cols]
                for col_tap in range(3)
            ],
            axis=0,
        )
        flat_weight = weight[row_tap].reshape(3 * inputs, outputs)
        term = jnp.einsum("cm,czhw->mzhw", flat_weight, stacked, preferred_element_type=jnp.float32)
        total = term if total is None else total + term
    return total


def depth_conv(padded, weight):
    depth = padded.shape[1] - 2
    stacked = jnp.stack([padded[:, tap : tap + depth] for tap in range(3)], axis=0)
    return jnp.einsum("kom,kmzhw->ozhw", weight, stacked, preferred_element_type=jnp.float32)


def pad_plane(field):
    return jnp.pad(field, ((0, 0), (0, 0), (1, 1), (1, 1)))


def pad_columns(field):
    return jnp.pad(field, ((0, 0), (0, 0), (0, 0), (1, 1)))


def local(volume, plane_weight, depth_weight, grad_out):
    filt_index = lax.axis_index("filt")
    partial_mid = plane_conv(pad_plane(volume), plane_weight)
    mid = lax.psum_scatter(partial_mid, "chan", scatter_dimension=2, tiled=True).astype(
        jnp.bfloat16
    )
    out_count = grad_out.shape[0]
    mid_count = mid.shape[0]
    forward_weight = lax.dynamic_slice_in_dim(depth_weight, filt_index * out_count, out_count, 1)
    own_columns = lax.dynamic_slice_in_dim(depth_weight, filt_index * mid_count, mid_count, 2)
    backward_weight = jnp.transpose(own_columns[::-1], (0, 2, 1))
    whole_mid = lax.all_gather(mid, "filt", axis=0, tiled=True)
    padded_mid = with_halo(whole_mid, (("slab", 1),), 1)
    output = depth_conv(padded_mid, forward_weight).astype(jnp.bfloat16)
    whole_grad = lax.all_gather(grad_out, "filt", axis=0, tiled=True)
    padded_grad = with_halo(whole_grad, (("slab", 1),), 1)
    grad_mid = depth_conv(padded_grad, backward_weight).astype(jnp.bfloat16)
    tall_grad = lax.all_gather(grad_mid, "chan", axis=2, tiled=True)
    turned = lax.all_to_all(tall_grad, "filt", split_axis=2, concat_axis=0, tiled=True)
    rimmed_grad = with_halo(turned, (("filt", 2),), 1)
    all_mid_weight = lax.all_gather(plane_weight, "filt", axis=3, tiled=True)
    flipped = jnp.transpose(all_mid_weight[::-1, ::-1], (0, 1, 3, 2))
    grad_in = plane_conv(pad_columns(rimmed_grad), flipped).astype(jnp.bfloat16)
    return (output, grad_in)


def solution(mesh):
    placed = (
        P("chan", "slab", None, None),
        P(None, None, "chan", "filt"),
        P(),
        P("filt", "slab", "chan", None),
    )
    return jax.shard_map(
        local,
        mesh=mesh,
        in_specs=placed,
        out_specs=(P("filt", "slab", "chan", None), P("chan", "slab", "filt", None)),
        check_vma=False,
    )
```

profile of v0, /device:TPU:9, one launch (start us, length us, event | category | flops | bytes accessed | tf_op | source)
XLA Modules:
  0.0 231.1 jit_solution(7157435260248938483)
XLA Ops:
  8.1 2.1 copy.65
  10.2 3.0 %copy.58 = bf16[128,2,32,128]{3,0,2,1:T(8,128)(2,1)S(1)} copy(bf16[128,2,32,128]{3,2,1,0:T(8,128)(2,1)} %param.4) | data formatting | bytes 4194304 | tf_op args[0]
  13.5 4.0 %pad_slice_fusion.2 = (bf16[128,2,32,128]{3,0,2,1:T(8,128)(2,1)S(1)}, bf16[128,2,32,128]{3,0,2,1:T(8,128)(2,1)S(1)}, bf16[128,2,32,128]{3,0,2,1:T(8,128)(2,1)S(1...) fusion(bf16[128,2,32,128]{3,0,2,1:T(8,128)(2,1)S(1)} %copy.58), kind=kLoop, calls=%fused_computation.2 | loop fusion | bytes 18874368 | tf_op jit(solution)/shard_map/slice | solution.py:29
  17.5 1.7 fusion.6
  19.2 1.7 fusion
  20.9 1.7 add_bitcast_fusion
  22.7 2.6 %copy.99 = f32[4,8,128,128]{3,1,2,0:T(8,128)} copy(f32[4,8,128,128]{3,2,1,0:T(8,128)S(1)} %bitcast.96) | data formatting | bytes 4194304
  25.4 31.0 %all-gather.6.cloned.1.call-done = bf16[256,2,16,128]{3,0,2,1:T(8,128)(2,1)} async-done(((bf16[64,2,16,128]{3,0,2,1:T(8,128)(2,1)}), bf16[256,2,16,128]{3,0,2,1:T(8,128)(2,1)}) %all-gather.6.cloned.1.call-update) | async-done | bytes 2097168 | tf_op jit(solution)/shard_map/all_gather | solution.py:68
  56.3 2.9 %fusion.95 = (bf16[256,1,16,128]{3,0,2,1:T(8,128)(2,1)}, bf16[256,1,16,128]{3,0,2,1:T(8,128)(2,1)S(1)}) fusion(bf16[256,2,16,128]{3,0,2,1:T(8,128)(2,1)} %all-gather.6.cloned.1.call-done), kind=kLoop, calls=%fused_computation.96 | loop fusion | bytes 4194304 | tf_op jit(solution)/shard_map/slice | solution.py:12
  59.3 3.9 %collective-permute-start.2 = (bf16[256,1,16,128]{3,0,2,1:T(8,128)(2,1)}, bf16[256,1,16,128]{3,0,2,1:T(8,128)(2,1)}, u32[]{:S(2)}, u32[]{:S(2)}) collective-permute-start(bf16[256,1,16,128]{3,0,2,1:T(8,128)(2,1)} %get-tuple-element.12), channel_id=1, source_target_pairs={{0,8},{8,16},{16,24},{1,9},{9,17},{17,25},{2,10},{10,18},{18,26},{... | collective-permute-start | bytes 3145736 | tf_op jit(solution)/shard_map/ppermute | solution.py:14
  63.2 1.9 collective-permute-start.3
  65.9 1.6 rev.6
  67.5 7.7 %collective-permute-done.2 = bf16[256,1,16,128]{3,0,2,1:T(8,128)(2,1)} collective-permute-done((bf16[256,1,16,128]{3,0,2,1:T(8,128)(2,1)}, bf16[256,1,16,128]{3,0,2,1:T(8,128)(2,1)}, u32[]{:S(2)}, u32[]{:S(2)}) %collective-permute-start.2) | collective-permute-done | bytes 1048608 | tf_op jit(solution)/shard_map/ppermute | solution.py:14
  75.2 4.2 %collective-permute-done.3 = bf16[256,1,16,128]{3,0,2,1:T(8,128)(2,1)} collective-permute-done((bf16[256,1,16,128]{3,0,2,1:T(8,128)(2,1)S(1)}, bf16[256,1,16,128]{3,0,2,1:T(8,128)(2,1)}, u32[]{:S(2)}, u32[]{:S(2)}) %collective-permute-start.3) | collective-permute-done | bytes 1048608 | tf_op jit(solution)/shard_map/ppermute | solution.py:15
  79.4 1.9 fusion.46
  81.3 2.1 fusion.74
  85.8 17.6 %all-gather.8.cloned.1.call-done = bf16[64,2,32,128]{3,0,2,1:T(8,128)(2,1)} async-done(((bf16[64,2,16,128]{3,0,2,1:T(8,128)(2,1)}), bf16[64,2,32,128]{3,0,2,1:T(8,128)(2,1)}) %all-gather.8.cloned.1.call-update) | async-done | bytes 1048592 | tf_op jit(solution)/shard_map/all_gather | solution.py:71
  103.5 2.3 copy.69
  105.8 4.6 %all-to-all-start = ((bf16[64,2,32,128]{3,0,1,2:T(8,128)(2,1)}), bf16[64,2,32,128]{3,0,1,2:T(8,128)(2,1)S(1)}, u32[]{:S(2)}, u32[]{:S(2)}) async-start(bf16[64,2,32,128]{3,0,1,2:T(8,128)(2,1)} %copy.69), calls=%async_computation | async-start | bytes 2097152 | tf_op jit(solution)/shard_map/all_to_all | solution.py:72
  110.4 64.2 %all_gather.15 = bf16[3,3,128,256]{2,3,1,0:T(8,128)(2,1)S(1)} all-gather(bf16[3,3,128,64]{2,3,1,0:T(8,128)(2,1)S(1)} %copy-done.9), channel_id=1, replica_groups=mesh['slab'=4,'chan'=2,'filt'=4] {'filt'}, dimensions={3}, use_global_device_ids=true | all-gather | bytes 737280 | tf_op jit(solution)/shard_map/all_gather | solution.py:74
  177.0 1.9 collective-permute-start.5
  178.9 3.4 %collective-permute-start.4 = (bf16[256,2,1,128]{0,3,2,1:T(8,128)(2,1)S(1)}, bf16[256,2,1,128]{0,3,2,1:T(8,128)(2,1)S(1)}, u32[]{:S(2)}, u32[]{:S(2)}) collective-permute-start(bf16[256,2,1,128]{0,3,2,1:T(8,128)(2,1)S(1)} %get-tuple-element.32), channel_id=1, source_target_pairs={{0,1},{1,2},{2,3},{4,5},{5,6},{6,7},{8,9},{9,10},{10,11},{12,13},{... | collective-permute-start | bytes 393224 | tf_op jit(solution)/shard_map/ppermute | solution.py:14
  183.1 1.5 collective-permute-done.4
  186.0 3.2 %fusion.97 = (bf16[256,2,8,128]{0,3,2,1:T(8,128)(2,1)}, bf16[256,2,8,128]{0,3,2,1:T(8,128)(2,1)S(1)}, bf16[256,2,8,128]{0,3,2,1:T(8,128)(2,1)}, bf16[256,2,8,128...) fusion(bf16[256,2,10,130]{0,3,2,1:T(8,128)(2,1)S(1)} %fusion.55), kind=kLoop, calls=%fused_computation.98 | loop fusion | bytes 12582912 | tf_op jit(solution)/shard_map/slice | solution.py:29
  189.2 3.3 %fusion.96 = (bf16[256,1,16,128]{3,0,2,1:T(8,128)(2,1)}, bf16[256,1,16,128]{3,0,2,1:T(8,128)(2,1)}) fusion(bf16[256,2,16,128]{3,0,2,1:T(8,128)(2,1)} %all-gather.4.cloned.1.call-done), kind=kLoop, calls=%fused_computation.97 | loop fusion | bytes 4194304 | tf_op jit(solution)/shard_map/slice | solution.py:12
  192.5 10.1 %collective-permute-start = (bf16[256,1,16,128]{3,0,2,1:T(8,128)(2,1)}, bf16[256,1,16,128]{3,0,2,1:T(8,128)(2,1)}, u32[]{:S(2)}, u32[]{:S(2)}) collective-permute-start(bf16[256,1,16,128]{3,0,2,1:T(8,128)(2,1)} %get-tuple-element.16), channel_id=1, source_target_pairs={{0,8},{8,16},{16,24},{1,9},{9,17},{17,25},{2,10},{10,18},{18,26},{... | collective-permute-start | bytes 3145736 | tf_op jit(solution)/shard_map/ppermute | solution.py:14
  202.6 2.1 collective-permute-start.1
  207.6 1.9 fusion.77
  209.5 2.2 copy.79
  211.7 2.9 %collective-permute-done = bf16[256,1,16,128]{3,0,2,1:T(8,128)(2,1)} collective-permute-done((bf16[256,1,16,128]{3,0,2,1:T(8,128)(2,1)}, bf16[256,1,16,128]{3,0,2,1:T(8,128)(2,1)}, u32[]{:S(2)}, u32[]{:S(2)}) %collective-permute-start) | collective-permute-done | bytes 1048608 | tf_op jit(solution)/shard_map/ppermute | solution.py:14
  214.7 4.4 %collective-permute-done.1 = bf16[256,1,16,128]{3,0,2,1:T(8,128)(2,1)} collective-permute-done((bf16[256,1,16,128]{3,0,2,1:T(8,128)(2,1)}, bf16[256,1,16,128]{3,0,2,1:T(8,128)(2,1)}, u32[]{:S(2)}, u32[]{:S(2)}) %collective-permute-start.1) | collective-permute-done | bytes 1048608 | tf_op jit(solution)/shard_map/ppermute | solution.py:15
  219.1 1.9 fusion.48
  (69 shorter events, 13.6 us)
Async XLA Ops:
  8.0 57.1 %copy-start = (bf16[3,256,256]{2,1,0:T(8,128)(2,1)S(1)}, bf16[3,256,256]{2,1,0:T(8,128)(2,1)}, u32[]{:S(2)}) copy-start(bf16[3,256,256]{2,1,0:T(8,128)(2,1)} %param.6) | copy-start | bytes 1179652
  8.0 48.3 %all-gather.6.cloned.1.call-start = ((), (), s32[]{:S(2)}) async-start(), calls=%async_computation.3 | async-start | bytes 2621440 | tf_op jit(solution)/shard_map/all_gather | solution.py:68
  10.2 3.0 %copy-start.8 = (bf16[3,3,128,64]{2,3,1,0:T(8,128)(2,1)S(1)}, bf16[3,3,128,64]{2,3,1,0:T(8,128)(2,1)}, u32[]{:S(2)}) copy-start(bf16[3,3,128,64]{2,3,1,0:T(8,128)(2,1)} %param.5) | copy-start | bytes 442372
  10.2 73.4 %reduce-scatter.5.cloned.1.call-start = ((), (), s32[]{:S(2)}) async-start(), calls=%async_computation.5 | async-start | bytes 3145728
  25.3 78.2 %all-gather.8.cloned.1.call-start = ((), (), s32[]{:S(2)}) async-start(), calls=%async_computation.4 | async-start | bytes 1572864 | tf_op jit(solution)/shard_map/all_gather | solution.py:71
  56.3 23.1 %copy-start.1 = (bf16[256,2,16,128]{3,0,2,1:T(8,128)(2,1)S(1)}, bf16[256,2,16,128]{3,0,2,1:T(8,128)(2,1)}, u32[]{:S(2)}) copy-start(bf16[256,2,16,128]{3,0,2,1:T(8,128)(2,1)} %all-gather.6.cloned.1.call-done) | copy-start | bytes 6291460
  59.3 15.9 %collective-permute-start.2 = (bf16[256,1,16,128]{3,0,2,1:T(8,128)(2,1)}, bf16[256,1,16,128]{3,0,2,1:T(8,128)(2,1)}, u32[]{:S(2)}, u32[]{:S(2)}) collective-permute-start(bf16[256,1,16,128]{3,0,2,1:T(8,128)(2,1)} %get-tuple-element.12), channel_id=1, source_target_pairs={{0,8},{8,16},{16,24},{1,9},{9,17},{17,25},{2,10},{10,18},{18,26},{... | collective-permute-start | bytes 3145736 | tf_op jit(solution)/shard_map/ppermute | solution.py:14
  63.2 16.2 %collective-permute-start.3 = (bf16[256,1,16,128]{3,0,2,1:T(8,128)(2,1)S(1)}, bf16[256,1,16,128]{3,0,2,1:T(8,128)(2,1)}, u32[]{:S(2)}, u32[]{:S(2)}) collective-permute-start(bf16[256,1,16,128]{3,0,2,1:T(8,128)(2,1)S(1)} %get-tuple-element.13), channel_id=1, source_target_pairs={{8,0},{16,8},{24,16},{9,1},{17,9},{25,17},{10,2},{18,10},{26,18},{... | collective-permute-start | bytes 3145736 | tf_op jit(solution)/shard_map/ppermute | solution.py:15
  67.5 13.8 %copy-start.13 = (bf16[3,256,64]{2,1,0:T(8,128)(2,1)S(1)}, bf16[3,256,64]{2,1,0:T(8,128)(2,1)}, u32[]{:S(2)}) copy-start(bf16[3,256,64]{2,1,0:T(8,128)(2,1)} %rev.6) | copy-start | bytes 294916
  83.5 105.7 %all-gather.4.cloned.1.call-start = ((), (), s32[]{:S(2)}) async-start(), calls=%async_computation.2 | async-start | bytes 2621440 | tf_op jit(solution)/shard_map/all_gather | solution.py:65
  85.8 24.5 %copy-start.9 = (bf16[3,3,128,64]{2,3,1,0:T(8,128)(2,1)S(1)}, bf16[3,3,128,64]{2,3,1,0:T(8,128)(2,1)}, u32[]{:S(2)}) copy-start(bf16[3,3,128,64]{2,3,1,0:T(8,128)(2,1)} %param.5) | copy-start | bytes 442372
  105.8 69.7 %all-to-all-start = ((bf16[64,2,32,128]{3,0,1,2:T(8,128)(2,1)}), bf16[64,2,32,128]{3,0,1,2:T(8,128)(2,1)S(1)}, u32[]{:S(2)}, u32[]{:S(2)}) async-start(bf16[64,2,32,128]{3,0,1,2:T(8,128)(2,1)} %copy.69), calls=%async_computation | async-start | bytes 2097152 | tf_op jit(solution)/shard_map/all_to_all | solution.py:72
  176.1 6.1 %copy-start.3 = (bf16[3,3,256,128]{3,2,1,0:T(8,128)(2,1)S(1)}, bf16[3,3,256,128]{3,2,1,0:T(8,128)(2,1)}, u32[]{:S(2)}) copy-start(bf16[3,3,256,128]{3,2,1,0:T(8,128)(2,1)} %reverse_bitcast_fusion) | copy-start | bytes 1769476
  177.0 6.1 %collective-permute-start.5 = (bf16[256,2,1,128]{0,3,2,1:T(8,128)(2,1)S(1)}, bf16[256,2,1,128]{0,3,2,1:T(8,128)(2,1)S(1)}, u32[]{:S(2)}, u32[]{:S(2)}) collective-permute-start(bf16[256,2,1,128]{0,3,2,1:T(8,128)(2,1)S(1)} %get-tuple-element.33), channel_id=1, source_target_pairs={{1,0},{2,1},{3,2},{5,4},{6,5},{7,6},{9,8},{10,9},{11,10},{13,12},{... | collective-permute-start | bytes 393224 | tf_op jit(solution)/shard_map/ppermute | solution.py:15
  178.9 5.7 %collective-permute-start.4 = (bf16[256,2,1,128]{0,3,2,1:T(8,128)(2,1)S(1)}, bf16[256,2,1,128]{0,3,2,1:T(8,128)(2,1)S(1)}, u32[]{:S(2)}, u32[]{:S(2)}) collective-permute-start(bf16[256,2,1,128]{0,3,2,1:T(8,128)(2,1)S(1)} %get-tuple-element.32), channel_id=1, source_target_pairs={{0,1},{1,2},{2,3},{4,5},{5,6},{6,7},{8,9},{9,10},{10,11},{12,13},{... | collective-permute-start | bytes 393224 | tf_op jit(solution)/shard_map/ppermute | solution.py:14
  183.1 1.5 copy-start.16
  184.6 0.7 copy-start.14
  189.2 15.6 %copy-start.6 = (bf16[256,2,8,128]{0,3,2,1:T(8,128)(2,1)S(1)}, bf16[256,2,8,128]{0,3,2,1:T(8,128)(2,1)}, u32[]{:S(2)}) copy-start(bf16[256,2,8,128]{0,3,2,1:T(8,128)(2,1)} %get-tuple-element.28) | copy-start | bytes 3145732
  189.2 15.6 %copy-start.7 = (bf16[256,2,8,128]{0,3,2,1:T(8,128)(2,1)S(1)}, bf16[256,2,8,128]{0,3,2,1:T(8,128)(2,1)}, u32[]{:S(2)}) copy-start(bf16[256,2,8,128]{0,3,2,1:T(8,128)(2,1)} %get-tuple-element.29) | copy-start | bytes 3145732
  189.2 15.6 %copy-start.12 = (bf16[1,3,256,128]{3,2,1,0:T(8,128)(2,1)S(1)}, bf16[1,3,256,128]{3,2,1,0:T(8,128)(2,1)}, u32[]{:S(2)}) copy-start(bf16[1,3,256,128]{3,2,1,0:T(8,128)(2,1)} %get-tuple-element.36) | copy-start | bytes 589828
  192.5 22.2 %collective-permute-start = (bf16[256,1,16,128]{3,0,2,1:T(8,128)(2,1)}, bf16[256,1,16,128]{3,0,2,1:T(8,128)(2,1)}, u32[]{:S(2)}, u32[]{:S(2)}) collective-permute-start(bf16[256,1,16,128]{3,0,2,1:T(8,128)(2,1)} %get-tuple-element.16), channel_id=1, source_target_pairs={{0,8},{8,16},{16,24},{1,9},{9,17},{17,25},{2,10},{10,18},{18,26},{... | collective-permute-start | bytes 3145736 | tf_op jit(solution)/shard_map/ppermute | solution.py:14
  202.6 16.4 %collective-permute-start.1 = (bf16[256,1,16,128]{3,0,2,1:T(8,128)(2,1)}, bf16[256,1,16,128]{3,0,2,1:T(8,128)(2,1)}, u32[]{:S(2)}, u32[]{:S(2)}) collective-permute-start(bf16[256,1,16,128]{3,0,2,1:T(8,128)(2,1)} %get-tuple-element.17), channel_id=1, source_target_pairs={{8,0},{16,8},{24,16},{9,1},{17,9},{25,17},{10,2},{18,10},{26,18},{... | collective-permute-start | bytes 3145736 | tf_op jit(solution)/shard_map/ppermute | solution.py:15
  204.8 1.2 copy-start.11
  204.8 1.2 copy-start.17
  206.0 1.2 copy-start.4
  206.0 1.5 copy-start.5
  206.0 1.5 copy-start.10
  206.0 1.6 copy-start.15
  207.6 11.5 %copy-start.2 = (bf16[256,2,16,128]{3,0,2,1:T(8,128)(2,1)S(1)}, bf16[256,2,16,128]{3,0,2,1:T(8,128)(2,1)}, u32[]{:S(2)}) copy-start(bf16[256,2,16,128]{3,0,2,1:T(8,128)(2,1)} %all-gather.4.cloned.1.call-done) | copy-start | bytes 6291460
Sparse Core Ops, SparseCore 0:
  11.1 45.2 all-gather.5
Sparse Core Ops, SparseCore 1:
  25.4 32.8 reduce-scatter.4
  83.5 19.9 all-gather.7
  105.6 70.7 all-gather.3
where the time goes:
time: 232 us; the launch traced here: 231 us
  waiting for transfers between devices  69.4 us (30%)
  blocking collectives  64.2 us (28%)
  local copies, waits for them, and re-layouts  36.1 us (16%)
  starting transfers between devices  28.1 us (12%)
  between operations  16 us (7%)
  matrix products  12.8 us (6%)
  other arithmetic  4.51 us (2%)
    all_gather x1, blocking collectives, local(): all_mid_weight = lax.all_gather(plane_weight, 'filt', axis=3, tiled=True)  64.2 us
    all_gather x1, waiting for transfers between devices, local(): whole_grad = lax.all_gather(grad_out, 'filt', axis=0, tiled=True)  31 us
    all_gather x1, waiting for transfers between devices, local(): tall_grad = lax.all_gather(grad_mid, 'chan', axis=2, tiled=True)  17.6 us
    ppermute x3, starting transfers between devices, with_halo(): before = lax.ppermute(last, axis, up)  17.4 us
    unnamed x44, local copies, waits for them, and re-layouts  14.5 us
    ppermute x3, waiting for transfers between devices, with_halo(): before = lax.ppermute(last, axis, up)  12.1 us
    dot_general x6, matrix products, plane_conv(): jnp.einsum('cm,czhw->mzhw', flat_weight, stacked, preferred_element_type=...  9.31 us
    ppermute x3, waiting for transfers between devices, with_halo(): after = lax.ppermute(leading, axis, down)  8.59 us
  transfers between devices with their start and end apart: 11, of which 7 were waited for; matrix products, arithmetic and copies ran while one was open for 18% of the time, Pallas kernels for 0%

commit v1 on v0

--- a/solution.py
+++ b/solution.py
@@ -2,6 +2,18 @@
 import jax.numpy as jnp
 from jax import lax
 from jax.sharding import PartitionSpec as P
+
+
+def split_up(shard, dim, size):
+    lengths = shard.shape
+    blocks = shard.reshape(*lengths[:dim], size, lengths[dim] // size, *lengths[dim + 1 :])
+    return jnp.moveaxis(blocks, dim, 0)
+
+
+def joined_along(blocks, dim):
+    blocks = jnp.moveaxis(blocks, 0, dim)
+    dims = blocks.shape
+    return blocks.reshape(*dims[:dim], dims[dim] * dims[dim + 1], *dims[dim + 2 :])
 
 
 def with_halo(value, sides, width):
@@ -69,7 +81,14 @@
     padded_grad = with_halo(whole_grad, (("slab", 1),), 1)
     grad_mid = depth_conv(padded_grad, backward_weight).astype(jnp.bfloat16)
     tall_grad = lax.all_gather(grad_mid, "chan", axis=2, tiled=True)
-    turned = lax.all_to_all(tall_grad, "filt", split_axis=2, concat_axis=0, tiled=True)
+    size_2, index = (lax.axis_size("filt"), lax.axis_index("filt"))
+    blocks = split_up(tall_grad, 2, size_2)
+    finished = [blocks[index]]
+    for step in range(1, size_2):
+        sent = blocks[index ^ step]
+        finished.append(lax.ppermute(sent, "filt", [(i_2, i_2 ^ step) for i_2 in range(size_2)]))
+    blocks = jnp.stack(finished)[index ^ jnp.arange(size_2)]
+    turned = joined_along(blocks, 0)
     rimmed_grad = with_halo(turned, (("filt", 2),), 1)
     all_mid_weight = lax.all_gather(plane_weight, "filt", axis=3, tiled=True)
     flipped = jnp.transpose(all_mid_weight[::-1, ::-1], (0, 1, 3, 2))

time: 232 us -> 211 us (0.909)
  blocking collectives: 64.2 us -> 11.9 us
  waiting for transfers between devices: 69.4 us -> 95.6 us
  starting transfers between devices: 28.1 us -> 32.7 us
    all_gather x1, blocking collectives: 64.2 us -> 11.9 us  [local(): all_mid_weight = lax.all_gather(plane_weight, 'filt', axis=3, tiled=True)]
    ppermute x0 -> x3, waiting for transfers between devices: none -> 35.6 us  [local(): lax.ppermute(sent, 'filt', [(i_2, i_2 ^ step) for i_2 in range(size_2)])]
    all_gather x1, waiting for transfers between devices: 17.6 us -> 5.76 us  [local(): tall_grad = lax.all_gather(grad_mid, 'chan', axis=2, tiled=True)]
    ppermute x3, starting transfers between devices: 5.94 us -> 14.4 us  [with_halo(): after = lax.ppermute(leading, axis, down)]
    all_to_all x1 -> x0, starting transfers between devices: 4.57 us -> none  [local(): lax.all_to_all(tall_grad, 'filt', split_axis=2, concat_axis=0, tiled=True)]
    ppermute x0 -> x3, starting transfers between devices: none -> 3.52 us  [local(): lax.ppermute(sent, 'filt', [(i_2, i_2 ^ step) for i_2 in range(size_2)])]
    ppermute x3, starting transfers between devices: 17.4 us -> 14.6 us  [with_halo(): before = lax.ppermute(last, axis, up)]
  transfers between devices with their start and end apart: 11 -> 13, of which waited for: 7 -> 10; matrix products, arithmetic and copies ran while one was open for 18% -> 20% of each run, Pallas kernels for 0% -> 0%
where the time goes in v1:
time: 211 us; the launch traced here: 209 us
  waiting for transfers between devices  95.6 us (45%)
  local copies, waits for them, and re-layouts  35.7 us (17%)
  starting transfers between devices  32.7 us (15%)
  between operations  16.1 us (8%)
  matrix products  12.8 us (6%)
  blocking collectives  11.9 us (6%)
  other arithmetic  4.65 us (2%)
    ppermute x3, waiting for transfers between devices, local(): lax.ppermute(sent, 'filt', [(i_2, i_2 ^ step) for i_2 in range(size_2)])  35.6 us
    all_gather x1, waiting for transfers between devices, local(): whole_grad = lax.all_gather(grad_out, 'filt', axis=0, tiled=True)  31 us
    ppermute x3, starting transfers between devices, with_halo(): before = lax.ppermute(last, axis, up)  14.6 us
    unnamed x44, local copies, waits for them, and re-layouts  14.5 us
    ppermute x3, starting transfers between devices, with_halo(): after = lax.ppermute(leading, axis, down)  14.4 us
    ppermute x3, waiting for transfers between devices, with_halo(): before = lax.ppermute(last, axis, up)  13 us
    all_gather x1, blocking collectives, local(): all_mid_weight = lax.all_gather(plane_weight, 'filt', axis=3, tiled=True)  11.9 us
    ppermute x3, waiting for transfers between devices, with_halo(): after = lax.ppermute(leading, axis, down)  10.2 us
  transfers between devices with their start and end apart: 13, of which 10 were waited for; matrix products, arithmetic and copies ran while one was open for 20% of the time, Pallas kernels for 0%

profile of v1, /device:TPU:9, one launch (start us, length us, event | category | flops | bytes accessed | tf_op | source)
XLA Modules:
  0.0 209.5 jit_solution(17764982691289297933)
XLA Ops:
  8.1 2.1 copy.47
  10.2 3.0 %copy.40 = bf16[128,2,32,128]{3,0,2,1:T(8,128)(2,1)S(1)} copy(bf16[128,2,32,128]{3,2,1,0:T(8,128)(2,1)} %param.4) | data formatting | bytes 4194304 | tf_op args[0]
  13.5 4.0 %pad_slice_fusion.2 = (bf16[128,2,32,128]{3,0,2,1:T(8,128)(2,1)S(1)}, bf16[128,2,32,128]{3,0,2,1:T(8,128)(2,1)S(1)}, bf16[128,2,32,128]{3,0,2,1:T(8,128)(2,1)S(1...) fusion(bf16[128,2,32,128]{3,0,2,1:T(8,128)(2,1)S(1)} %copy.40), kind=kLoop, calls=%fused_computation.3 | loop fusion | bytes 18874368 | tf_op jit(solution)/shard_map/slice | solution.py:41
  17.5 1.7 fusion.6
  19.2 1.7 fusion
  20.9 1.7 add_bitcast_fusion
  22.7 2.6 %copy.85 = f32[4,8,128,128]{3,1,2,0:T(8,128)} copy(f32[4,8,128,128]{3,2,1,0:T(8,128)S(1)} %bitcast.111) | data formatting | bytes 4194304
  25.4 31.0 %all-gather.6.cloned.1.call-done = bf16[256,2,16,128]{3,0,2,1:T(8,128)(2,1)} async-done(((bf16[64,2,16,128]{3,0,2,1:T(8,128)(2,1)}), bf16[256,2,16,128]{3,0,2,1:T(8,128)(2,1)}) %all-gather.6.cloned.1.call-update) | async-done | bytes 2097168 | tf_op jit(solution)/shard_map/all_gather | solution.py:80
  56.3 2.9 %fusion.96 = (bf16[256,1,16,128]{3,0,2,1:T(8,128)(2,1)}, bf16[256,1,16,128]{3,0,2,1:T(8,128)(2,1)S(1)}) fusion(bf16[256,2,16,128]{3,0,2,1:T(8,128)(2,1)} %all-gather.6.cloned.1.call-done), kind=kLoop, calls=%fused_computation.109 | loop fusion | bytes 4194304 | tf_op jit(solution)/shard_map/slice | solution.py:24
  59.3 3.9 %collective-permute-start.2 = (bf16[256,1,16,128]{3,0,2,1:T(8,128)(2,1)}, bf16[256,1,16,128]{3,0,2,1:T(8,128)(2,1)}, u32[]{:S(2)}, u32[]{:S(2)}) collective-permute-start(bf16[256,1,16,128]{3,0,2,1:T(8,128)(2,1)} %get-tuple-element.10), channel_id=1, source_target_pairs={{0,8},{8,16},{16,24},{1,9},{9,17},{17,25},{2,10},{10,18},{18,26},{... | collective-permute-start | bytes 3145736 | tf_op jit(solution)/shard_map/ppermute | solution.py:26
  63.2 1.9 collective-permute-start.3
  65.9 1.6 rev.6
  67.5 7.7 %collective-permute-done.2 = bf16[256,1,16,128]{3,0,2,1:T(8,128)(2,1)} collective-permute-done((bf16[256,1,16,128]{3,0,2,1:T(8,128)(2,1)}, bf16[256,1,16,128]{3,0,2,1:T(8,128)(2,1)}, u32[]{:S(2)}, u32[]{:S(2)}) %collective-permute-start.2) | collective-permute-done | bytes 1048608 | tf_op jit(solution)/shard_map/ppermute | solution.py:26
  75.2 4.4 %collective-permute-done.3 = bf16[256,1,16,128]{3,0,2,1:T(8,128)(2,1)} collective-permute-done((bf16[256,1,16,128]{3,0,2,1:T(8,128)(2,1)S(1)}, bf16[256,1,16,128]{3,0,2,1:T(8,128)(2,1)}, u32[]{:S(2)}, u32[]{:S(2)}) %collective-permute-start.3) | collective-permute-done | bytes 1048608 | tf_op jit(solution)/shard_map/ppermute | solution.py:27
  79.6 1.9 fusion.46
  81.5 2.1 %fusion.74 = bf16[64,2,16,128]{3,0,2,1:T(8,128)(2,1)} fusion(bf16[1,256,2,16,128]{4,1,0,3,2:T(8,128)(2,1)S(1)} %get-tuple-element.9, bf16[1,256,2,16,128]{4,1,0,3,2:T(8,128)(2,1)S(1)} %bitcast.113, bf16[1,256,2,16,128]{4,1,0,3,2:T(8,128)(2,1)S(1)} %get-tuple-element.8, bf16[3,256,64]{2,1,0:T(8,128)(2,1)S(1)} %copy-done.13), kind=kOutput, calls=%fused_computation.77 | convolution fusion | flops 421789696 | bytes 6914048 | tf_op jit(solution)/shard_map/kom,kmzhw->ozhw/dot_general | solution.py:55
  86.0 11.9 %all_gather.15 = bf16[3,3,128,256]{2,3,1,0:T(8,128)(2,1)S(1)} all-gather(bf16[3,3,128,64]{2,3,1,0:T(8,128)(2,1)S(1)} %copy-done.9), channel_id=1, replica_groups=mesh['slab'=4,'chan'=2,'filt'=4] {'filt'}, dimensions={3}, use_global_device_ids=true | all-gather | bytes 737280 | tf_op jit(solution)/shard_map/all_gather | solution.py:93
  97.9 5.8 %all-gather.8.cloned.1.call-done = bf16[64,2,32,128]{3,0,2,1:T(8,128)(2,1)} async-done(((bf16[64,2,16,128]{3,0,2,1:T(8,128)(2,1)}), bf16[64,2,32,128]{3,0,2,1:T(8,128)(2,1)}) %all-gather.8.cloned.1.call-update) | async-done | bytes 1048592 | tf_op jit(solution)/shard_map/all_gather | solution.py:83
  110.0 21.6 %collective-permute-done.6 = bf16[64,2,8,128]{3,2,1,0:T(8,128)(2,1)S(1)} collective-permute-done((bf16[64,2,8,128]{3,2,1,0:T(8,128)(2,1)S(1)}, bf16[64,2,8,128]{3,2,1,0:T(8,128)(2,1)S(1)}, u32[]{:S(2)}, u32[]{:S(2)}) %collective-permute-start.6) | collective-permute-done | bytes 262176 | tf_op jit(solution)/shard_map/ppermute | solution.py:89
  131.6 14.0 %collective-permute-done.5 = bf16[64,2,8,128]{3,2,1,0:T(8,128)(2,1)S(1)} collective-permute-done((bf16[64,2,8,128]{3,2,1,0:T(8,128)(2,1)S(1)}, bf16[64,2,8,128]{3,2,1,0:T(8,128)(2,1)S(1)}, u32[]{:S(2)}, u32[]{:S(2)}) %collective-permute-start.5) | collective-permute-done | bytes 262176 | tf_op jit(solution)/shard_map/ppermute | solution.py:89
  147.3 10.4 %collective-permute-start.8 = (bf16[256,2,1,128]{0,3,2,1:T(8,128)(2,1)S(1)}, bf16[256,2,1,128]{0,3,2,1:T(8,128)(2,1)S(1)}, u32[]{:S(2)}, u32[]{:S(2)}) collective-permute-start(bf16[256,2,1,128]{0,3,2,1:T(8,128)(2,1)S(1)} %get-tuple-element.31), channel_id=1, source_target_pairs={{1,0},{2,1},{3,2},{5,4},{6,5},{7,6},{9,8},{10,9},{11,10},{13,12},{... | collective-permute-start | bytes 393224 | tf_op jit(solution)/shard_map/ppermute | solution.py:27
  157.8 1.9 collective-permute-start.7
  161.9 2.4 %collective-permute-done.7 = bf16[256,2,1,128]{0,3,2,1:T(8,128)(2,1)S(1)} collective-permute-done((bf16[256,2,1,128]{0,3,2,1:T(8,128)(2,1)S(1)}, bf16[256,2,1,128]{0,3,2,1:T(8,128)(2,1)S(1)}, u32[]{:S(2)}, u32[]{:S(2)}) %collective-permute-start.7) | collective-permute-done | bytes 131104 | tf_op jit(solution)/shard_map/ppermute | solution.py:26
  165.7 3.2 %fusion.98 = (bf16[256,2,8,128]{0,3,2,1:T(8,128)(2,1)}, bf16[256,2,8,128]{0,3,2,1:T(8,128)(2,1)S(1)}, bf16[256,2,8,128]{0,3,2,1:T(8,128)(2,1)}, bf16[256,2,8,128...) fusion(bf16[256,2,10,130]{0,3,2,1:T(8,128)(2,1)S(1)} %fusion.55), kind=kLoop, calls=%fused_computation.111 | loop fusion | bytes 12582912 | tf_op jit(solution)/shard_map/slice | solution.py:41
  168.9 3.3 %fusion.97 = (bf16[256,1,16,128]{3,0,2,1:T(8,128)(2,1)}, bf16[256,1,16,128]{3,0,2,1:T(8,128)(2,1)}) fusion(bf16[256,2,16,128]{3,0,2,1:T(8,128)(2,1)} %all-gather.4.cloned.1.call-done), kind=kLoop, calls=%fused_computation.110 | loop fusion | bytes 4194304 | tf_op jit(solution)/shard_map/slice | solution.py:24
  172.2 8.8 %collective-permute-start = (bf16[256,1,16,128]{3,0,2,1:T(8,128)(2,1)}, bf16[256,1,16,128]{3,0,2,1:T(8,128)(2,1)}, u32[]{:S(2)}, u32[]{:S(2)}) collective-permute-start(bf16[256,1,16,128]{3,0,2,1:T(8,128)(2,1)} %get-tuple-element.14), channel_id=1, source_target_pairs={{0,8},{8,16},{16,24},{1,9},{9,17},{17,25},{2,10},{10,18},{18,26},{... | collective-permute-start | bytes 3145736 | tf_op jit(solution)/shard_map/ppermute | solution.py:26
  181.0 2.1 %collective-permute-start.1 = (bf16[256,1,16,128]{3,0,2,1:T(8,128)(2,1)}, bf16[256,1,16,128]{3,0,2,1:T(8,128)(2,1)}, u32[]{:S(2)}, u32[]{:S(2)}) collective-permute-start(bf16[256,1,16,128]{3,0,2,1:T(8,128)(2,1)} %get-tuple-element.15), channel_id=1, source_target_pairs={{8,0},{16,8},{24,16},{9,1},{17,9},{25,17},{10,2},{18,10},{26,18},{... | collective-permute-start | bytes 3145736 | tf_op jit(solution)/shard_map/ppermute | solution.py:27
  186.0 1.9 fusion.77
  187.9 2.2 %copy.62 = bf16[128,2,8,128]{3,2,1,0:T(8,128)(2,1)} copy(bf16[128,2,8,128]{0,3,2,1:T(8,128)(2,1)} %fusion.77) | data formatting | bytes 1048576
  190.1 2.9 %collective-permute-done = bf16[256,1,16,128]{3,0,2,1:T(8,128)(2,1)} collective-permute-done((bf16[256,1,16,128]{3,0,2,1:T(8,128)(2,1)}, bf16[256,1,16,128]{3,0,2,1:T(8,128)(2,1)}, u32[]{:S(2)}, u32[]{:S(2)}) %collective-permute-start) | collective-permute-done | bytes 1048608 | tf_op jit(solution)/shard_map/ppermute | solution.py:26
  193.0 4.4 %collective-permute-done.1 = bf16[256,1,16,128]{3,0,2,1:T(8,128)(2,1)} collective-permute-done((bf16[256,1,16,128]{3,0,2,1:T(8,128)(2,1)}, bf16[256,1,16,128]{3,0,2,1:T(8,128)(2,1)}, u32[]{:S(2)}, u32[]{:S(2)}) %collective-permute-start.1) | collective-permute-done | bytes 1048608 | tf_op jit(solution)/shard_map/ppermute | solution.py:27
  197.4 1.9 fusion.48
  (80 shorter events, 20.7 us)
Async XLA Ops:
  8.0 57.1 %copy-start = (bf16[3,256,256]{2,1,0:T(8,128)(2,1)S(1)}, bf16[3,256,256]{2,1,0:T(8,128)(2,1)}, u32[]{:S(2)}) copy-start(bf16[3,256,256]{2,1,0:T(8,128)(2,1)} %param.6) | copy-start | bytes 1179652
  8.0 48.3 %all-gather.6.cloned.1.call-start = ((), (), s32[]{:S(2)}) async-start(), calls=%async_computation.2 | async-start | bytes 2621440 | tf_op jit(solution)/shard_map/all_gather | solution.py:80
  10.2 3.0 %copy-start.8 = (bf16[3,3,128,64]{2,3,1,0:T(8,128)(2,1)S(1)}, bf16[3,3,128,64]{2,3,1,0:T(8,128)(2,1)}, u32[]{:S(2)}) copy-start(bf16[3,3,128,64]{2,3,1,0:T(8,128)(2,1)} %param.5) | copy-start | bytes 442372
  10.2 73.5 %reduce-scatter.5.cloned.1.call-start = ((), (), s32[]{:S(2)}) async-start(), calls=%async_computation.4 | async-start | bytes 3145728
  25.3 78.3 %all-gather.8.cloned.1.call-start = ((), (), s32[]{:S(2)}) async-start(), calls=%async_computation.3 | async-start | bytes 1572864 | tf_op jit(solution)/shard_map/all_gather | solution.py:83
  56.3 23.2 %copy-start.2 = (bf16[256,2,16,128]{3,0,2,1:T(8,128)(2,1)S(1)}, bf16[256,2,16,128]{3,0,2,1:T(8,128)(2,1)}, u32[]{:S(2)}) copy-start(bf16[256,2,16,128]{3,0,2,1:T(8,128)(2,1)} %all-gather.6.cloned.1.call-done) | copy-start | bytes 6291460
  59.3 15.9 %collective-permute-start.2 = (bf16[256,1,16,128]{3,0,2,1:T(8,128)(2,1)}, bf16[256,1,16,128]{3,0,2,1:T(8,128)(2,1)}, u32[]{:S(2)}, u32[]{:S(2)}) collective-permute-start(bf16[256,1,16,128]{3,0,2,1:T(8,128)(2,1)} %get-tuple-element.10), channel_id=1, source_target_pairs={{0,8},{8,16},{16,24},{1,9},{9,17},{17,25},{2,10},{10,18},{18,26},{... | collective-permute-start | bytes 3145736 | tf_op jit(solution)/shard_map/ppermute | solution.py:26
  63.2 16.4 %collective-permute-start.3 = (bf16[256,1,16,128]{3,0,2,1:T(8,128)(2,1)S(1)}, bf16[256,1,16,128]{3,0,2,1:T(8,128)(2,1)}, u32[]{:S(2)}, u32[]{:S(2)}) collective-permute-start(bf16[256,1,16,128]{3,0,2,1:T(8,128)(2,1)S(1)} %get-tuple-element.11), channel_id=1, source_target_pairs={{8,0},{16,8},{24,16},{9,1},{17,9},{25,17},{10,2},{18,10},{26,18},{... | collective-permute-start | bytes 3145736 | tf_op jit(solution)/shard_map/ppermute | solution.py:27
  67.5 14.0 %copy-start.13 = (bf16[3,256,64]{2,1,0:T(8,128)(2,1)S(1)}, bf16[3,256,64]{2,1,0:T(8,128)(2,1)}, u32[]{:S(2)}) copy-start(bf16[3,256,64]{2,1,0:T(8,128)(2,1)} %rev.6) | copy-start | bytes 294916
  83.6 2.4 %copy-start.9 = (bf16[3,3,128,64]{2,3,1,0:T(8,128)(2,1)S(1)}, bf16[3,3,128,64]{2,3,1,0:T(8,128)(2,1)}, u32[]{:S(2)}) copy-start(bf16[3,3,128,64]{2,3,1,0:T(8,128)(2,1)} %param.5) | copy-start | bytes 442372
  83.6 85.3 %all-gather.4.cloned.1.call-start = ((), (), s32[]{:S(2)}) async-start(), calls=%async_computation.1 | async-start | bytes 2621440 | tf_op jit(solution)/shard_map/all_gather | solution.py:77
  105.1 26.5 %collective-permute-start.6 = (bf16[64,2,8,128]{3,2,1,0:T(8,128)(2,1)S(1)}, bf16[64,2,8,128]{3,2,1,0:T(8,128)(2,1)S(1)}, u32[]{:S(2)}, u32[]{:S(2)}) collective-permute-start(bf16[64,2,8,128]{3,2,1,0:T(8,128)(2,1)S(1)} %bitcast.119), channel_id=1, source_target_pairs={{0,3},{1,2},{2,1},{3,0},{4,7},{5,6},{6,5},{7,4},{8,11},{9,10},{10,... | collective-permute-start | bytes 786440 | tf_op jit(solution)/shard_map/ppermute | solution.py:89
  106.5 39.1 %collective-permute-start.5 = (bf16[64,2,8,128]{3,2,1,0:T(8,128)(2,1)S(1)}, bf16[64,2,8,128]{3,2,1,0:T(8,128)(2,1)S(1)}, u32[]{:S(2)}, u32[]{:S(2)}) collective-permute-start(bf16[64,2,8,128]{3,2,1,0:T(8,128)(2,1)S(1)} %bitcast.120), channel_id=1, source_target_pairs={{0,2},{1,3},{2,0},{3,1},{4,6},{5,7},{6,4},{7,5},{8,10},{9,11},{10,... | collective-permute-start | bytes 786440 | tf_op jit(solution)/shard_map/ppermute | solution.py:89
  107.9 37.7 %collective-permute-start.4 = (bf16[64,2,8,128]{3,2,1,0:T(8,128)(2,1)S(1)}, bf16[64,2,8,128]{3,2,1,0:T(8,128)(2,1)S(1)}, u32[]{:S(2)}, u32[]{:S(2)}) collective-permute-start(bf16[64,2,8,128]{3,2,1,0:T(8,128)(2,1)S(1)} %bitcast.121), channel_id=1, source_target_pairs={{0,1},{1,0},{2,3},{3,2},{4,5},{5,4},{6,7},{7,6},{8,9},{9,8},{10,11... | collective-permute-start | bytes 786440 | tf_op jit(solution)/shard_map/ppermute | solution.py:89
  146.5 13.2 %copy-start.3 = (bf16[3,3,256,128]{3,2,1,0:T(8,128)(2,1)S(1)}, bf16[3,3,256,128]{3,2,1,0:T(8,128)(2,1)}, u32[]{:S(2)}) copy-start(bf16[3,3,256,128]{3,2,1,0:T(8,128)(2,1)} %reverse_bitcast_fusion) | copy-start | bytes 1769476
  147.3 14.6 %collective-permute-start.8 = (bf16[256,2,1,128]{0,3,2,1:T(8,128)(2,1)S(1)}, bf16[256,2,1,128]{0,3,2,1:T(8,128)(2,1)S(1)}, u32[]{:S(2)}, u32[]{:S(2)}) collective-permute-start(bf16[256,2,1,128]{0,3,2,1:T(8,128)(2,1)S(1)} %get-tuple-element.31), channel_id=1, source_target_pairs={{1,0},{2,1},{3,2},{5,4},{6,5},{7,6},{9,8},{10,9},{11,10},{13,12},{... | collective-permute-start | bytes 393224 | tf_op jit(solution)/shard_map/ppermute | solution.py:27
  157.8 6.6 %collective-permute-start.7 = (bf16[256,2,1,128]{0,3,2,1:T(8,128)(2,1)S(1)}, bf16[256,2,1,128]{0,3,2,1:T(8,128)(2,1)S(1)}, u32[]{:S(2)}, u32[]{:S(2)}) collective-permute-start(bf16[256,2,1,128]{0,3,2,1:T(8,128)(2,1)S(1)} %get-tuple-element.30), channel_id=1, source_target_pairs={{0,1},{1,2},{2,3},{4,5},{5,6},{6,7},{8,9},{9,10},{10,11},{12,13},{... | collective-permute-start | bytes 393224 | tf_op jit(solution)/shard_map/ppermute | solution.py:26
  161.9 2.4 %copy-start.16 = (bf16[256,2,1,128]{0,3,2,1:T(8,128)(2,1)}, bf16[256,2,1,128]{0,3,2,1:T(8,128)(2,1)S(1)}, u32[]{:S(2)}) copy-start(bf16[256,2,1,128]{0,3,2,1:T(8,128)(2,1)S(1)} %collective-permute-done.8) | copy-start | bytes 393220
  164.4 0.7 copy-start.14
  168.9 14.2 %copy-start.6 = (bf16[256,2,8,128]{0,3,2,1:T(8,128)(2,1)S(1)}, bf16[256,2,8,128]{0,3,2,1:T(8,128)(2,1)}, u32[]{:S(2)}) copy-start(bf16[256,2,8,128]{0,3,2,1:T(8,128)(2,1)} %get-tuple-element.26) | copy-start | bytes 3145732
  168.9 14.2 %copy-start.7 = (bf16[256,2,8,128]{0,3,2,1:T(8,128)(2,1)S(1)}, bf16[256,2,8,128]{0,3,2,1:T(8,128)(2,1)}, u32[]{:S(2)}) copy-start(bf16[256,2,8,128]{0,3,2,1:T(8,128)(2,1)} %get-tuple-element.27) | copy-start | bytes 3145732
  168.9 14.2 %copy-start.12 = (bf16[1,3,256,128]{3,2,1,0:T(8,128)(2,1)S(1)}, bf16[1,3,256,128]{3,2,1,0:T(8,128)(2,1)}, u32[]{:S(2)}) copy-start(bf16[1,3,256,128]{3,2,1,0:T(8,128)(2,1)} %get-tuple-element.38) | copy-start | bytes 589828
  172.2 20.8 %collective-permute-start = (bf16[256,1,16,128]{3,0,2,1:T(8,128)(2,1)}, bf16[256,1,16,128]{3,0,2,1:T(8,128)(2,1)}, u32[]{:S(2)}, u32[]{:S(2)}) collective-permute-start(bf16[256,1,16,128]{3,0,2,1:T(8,128)(2,1)} %get-tuple-element.14), channel_id=1, source_target_pairs={{0,8},{8,16},{16,24},{1,9},{9,17},{17,25},{2,10},{10,18},{18,26},{... | collective-permute-start | bytes 3145736 | tf_op jit(solution)/shard_map/ppermute | solution.py:26
  181.0 16.4 %collective-permute-start.1 = (bf16[256,1,16,128]{3,0,2,1:T(8,128)(2,1)}, bf16[256,1,16,128]{3,0,2,1:T(8,128)(2,1)}, u32[]{:S(2)}, u32[]{:S(2)}) collective-permute-start(bf16[256,1,16,128]{3,0,2,1:T(8,128)(2,1)} %get-tuple-element.15), channel_id=1, source_target_pairs={{8,0},{16,8},{24,16},{9,1},{17,9},{25,17},{10,2},{18,10},{26,18},{... | collective-permute-start | bytes 3145736 | tf_op jit(solution)/shard_map/ppermute | solution.py:27
  183.1 1.2 copy-start.11
  183.1 1.2 copy-start.17
  184.4 1.2 copy-start.4
  184.4 1.5 copy-start.5
  184.4 1.5 copy-start.10
  184.4 1.6 copy-start.15
  185.9 11.5 %copy-start.1 = (bf16[256,2,16,128]{3,0,2,1:T(8,128)(2,1)S(1)}, bf16[256,2,16,128]{3,0,2,1:T(8,128)(2,1)}, u32[]{:S(2)}) copy-start(bf16[256,2,16,128]{3,0,2,1:T(8,128)(2,1)} %all-gather.4.cloned.1.call-done) | copy-start | bytes 6291460
Sparse Core Ops, SparseCore 0:
  11.1 45.2 all-gather.5
Sparse Core Ops, SparseCore 1:
  25.4 32.8 reduce-scatter.4
  83.7 19.9 all-gather.7
  105.8 58.9 all-gather.3
